TPU v7x, 512 devices: a whole 4x4x16 slice. The times are simulated.
512 devices in a mesh: pipe: 4 (over y), expert: 32 (over z, core), tensor: 4 (over x).
Axes of the slice: x: 4, y: 4, z: 16, core: 2. Of those that a mesh axis runs over, the one named last changes fastest.
Arguments:
- tokens: bfloat16 [512, 6144], P('expert', ('pipe', 'tensor')), may hold values from -6 to 6
- expert_ids: int32 [512, 2], P('expert'), may hold values from 0 to 7, all different within a row; in each aligned block of 16 rows (0 to 15, 16 to 31, ...) at most 5 rows name the same one
- gates: float32 [512, 2], P('expert'), may hold values from 0.2 to 1
- w_gate: bfloat16 [32, 6144, 2048], P('expert', None, ('pipe', 'tensor')), may hold values from -0.078125 to 0.078125
- w_up: bfloat16 [32, 6144, 2048], P('expert', None, ('pipe', 'tensor')), may hold values from -0.078125 to 0.078125
- w_down: bfloat16 [32, 2048, 6144], P('expert', ('pipe', 'tensor')), may hold values from -0.0625 to 0.0625
- d_out: bfloat16 [512, 6144], P('expert', ('pipe', 'tensor')), may hold values from -6 to 6
Outputs:
- moe_out: bfloat16 [512, 6144], P('expert', ('pipe', 'tensor'))
- grad_tokens: bfloat16 [512, 6144], P('expert', ('pipe', 'tensor'))
- grad_gates: float32 [512, 2], P('expert')
Inputs may be any that keep to these rules, and one draw needn't show every extreme that they name: `expert_ids`: each row names 2 different experts. Among the rows of one index of expert (aligned blocks of 16 rows) no expert is named more than 5 times, a bound that some block reaches.
All inputs are finite; a program needn't handle non-finite values.
Results may differ from a plain program's by a relative error of at most 0.017.
Values may be sent and summed in bfloat16 or wider, within the bound.
No kernel may reach another device: no remote copies, remote signals or barrier semaphores. Data moves between devices by JAX's collectives and lax.ppermute only.
A program may use at most 64 MiB of HBM per device.

v0:
```python
import jax
import jax.numpy as jnp
from jax import lax
from jax.sharding import PartitionSpec as P


def per_device(tokens, expert_ids, gates, w_gate, w_up, w_down, d_out):
    tok_rows = tokens.shape[0]
    feat = tokens.shape[1]
    top = expert_ids.shape[1]
    devices_all = lax.axis_size("expert")
    experts = min(8, devices_all)
    group = devices_all // experts
    capacity = min(
        tok_rows,
        max(2, max(5 * tok_rows * top // (4 * experts), (tok_rows * top + experts - 1) // experts)),
    )
    slots = experts * capacity
    flat_ids = expert_ids.reshape(-1)
    onehot = (flat_ids[:, None] == jnp.arange(experts, dtype=jnp.int32)[None, :]).astype(jnp.int32)
    position = jnp.sum(jnp.cumsum(onehot, axis=0) * onehot, axis=1) - 1
    slot_of = flat_ids * capacity + position
    picks = (jnp.arange(slots, dtype=jnp.int32)[:, None] == slot_of[None, :]).astype(jnp.float32)
    pick_rows = picks.reshape(slots, tok_rows, top)
    select_tok = jnp.sum(pick_rows, axis=2).astype(jnp.bfloat16)
    select_gate = jnp.sum(pick_rows * gates[None, :, :], axis=2)
    picked = jnp.dot(select_tok, tokens, preferred_element_type=jnp.float32).astype(jnp.bfloat16)
    scaled = jnp.dot(
        select_gate, d_out.astype(jnp.float32), precision=lax.Precision.HIGHEST
    ).astype(jnp.bfloat16)
    send = jnp.concatenate([picked, scaled], axis=1).reshape(experts, capacity, 2 * feat)
    send = jnp.repeat(send, group, axis=0)
    recv = lax.all_to_all(send, "expert", split_axis=0, concat_axis=0, tiled=True)
    recv = recv.reshape(devices_all * capacity, 2 * feat)
    part_x = recv[:, :feat]
    part_dy = recv[:, feat:]
    rows_x = lax.all_gather(part_x, ("pipe", "tensor"), axis=1, tiled=True)
    rows_dy = lax.all_gather(part_dy, ("pipe", "tensor"), axis=1, tiled=True)
    gate_proj = w_gate[0]
    up_proj = w_up[0]
    down_proj = w_down[0]
    contract_last = (((1,), (1,)), ((), ()))
    h_gate = jnp.dot(rows_x, gate_proj, preferred_element_type=jnp.float32)
    h_up = jnp.dot(rows_x, up_proj, preferred_element_type=jnp.float32)
    sig = jax.nn.sigmoid(h_gate)
    hidden = (h_gate * sig * h_up).astype(jnp.bfloat16)
    out_terms = jnp.dot(hidden, down_proj, preferred_element_type=jnp.float32)
    d_hidden = lax.dot_general(
        rows_dy, down_proj, contract_last, preferred_element_type=jnp.float32
    )
    d_gate_h = (d_hidden * h_up * sig * (1.0 + h_gate * (1.0 - sig))).astype(jnp.bfloat16)
    d_up_h = (d_hidden * h_gate * sig).astype(jnp.bfloat16)
    dx_terms = lax.dot_general(
        d_gate_h, gate_proj, contract_last, preferred_element_type=jnp.float32
    )
    dx_terms = dx_terms + lax.dot_general(
        d_up_h, up_proj, contract_last, preferred_element_type=jnp.float32
    )
    out_share = lax.psum_scatter(
        out_terms.astype(jnp.bfloat16), ("pipe", "tensor"), scatter_dimension=1, tiled=True
    )
    dx_share = lax.psum_scatter(
        dx_terms.astype(jnp.bfloat16), ("pipe", "tensor"), scatter_dimension=1, tiled=True
    )
    back_send = jnp.concatenate([out_share, dx_share], axis=1).reshape(
        devices_all, capacity, 2 * feat
    )
    back = lax.all_to_all(back_send, "expert", split_axis=0, concat_axis=0, tiled=True)
    back_rows = (
        jnp.sum(back.astype(jnp.float32).reshape(experts, group, capacity, 2 * feat), axis=1)
        .astype(jnp.bfloat16)
        .reshape(slots, 2 * feat)
    )
    assign = picks.T.astype(jnp.bfloat16)
    a_both = jnp.dot(assign, back_rows, preferred_element_type=jnp.float32)
    a_out = a_both[:, :feat].reshape(tok_rows, top, feat)
    a_dx = a_both[:, feat:].reshape(tok_rows, top, feat)
    moe_out = jnp.sum(gates[:, :, None] * a_out, axis=1).astype(jnp.bfloat16)
    grad_tokens = jnp.sum(a_dx, axis=1).astype(jnp.bfloat16)
    partial_dots = jnp.sum(d_out.astype(jnp.float32)[:, None, :] * a_out, axis=2)
    grad_gates = lax.psum(partial_dots, ("pipe", "tensor"))
    return (moe_out, grad_tokens, grad_gates)


def solution(mesh):
    return jax.shard_map(
        per_device,
        mesh=mesh,
        in_specs=(
            P("expert", ("pipe", "tensor")),
            P("expert", None),
            P("expert", None),
            P("expert", None, ("pipe", "tensor")),
            P("expert", None, ("pipe", "tensor")),
            P("expert", ("pipe", "tensor"), None),
            P("expert", ("pipe", "tensor")),
        ),
        out_specs=(
            P("expert", ("pipe", "tensor")),
            P("expert", ("pipe", "tensor")),
            P("expert", None),
        ),
        check_vma=False,
    )
```

profile of v0, /device:TPU:32, one launch (start us, length us, event | category | flops | bytes accessed | tf_op | source)
XLA Modules:
  0.0 457.4 jit_solution(14242704866884179317)
XLA Ops:
  7.2 0.9 copy.35
  9.4 0.8 convert_reduce_fusion
  10.1 0.9 convolution_convert_fusion.1
  11.1 0.9 convolution_convert_fusion.2
  12.1 41.8 %all_to_all.10 = bf16[32,5,768]{2,1,0:T(8,128)(2,1)S(1)} all-to-all(bf16[32,5,768]{2,1,0:T(8,128)(2,1)S(1)} %bitcast.32), channel_id=1, replica_groups=mesh['pipe'=4,'expert'=32,'tensor'=4] {'expert'}, dimensions={0} | all-to-all | bytes 491520 | tf_op jit(solution)/shard_map/all_to_all | solution.py:33
  54.0 0.7 fusion.21
  55.6 54.5 %all-gather.3.cloned.1.call-done = bf16[160,6144]{1,0:T(8,128)(2,1)} async-done(((bf16[160,384]{1,0:T(8,128)(2,1)}), bf16[160,6144]{1,0:T(8,128)(2,1)}) %all-gather.3.cloned.1.call-update) | async-done | bytes 1966096 | tf_op jit(solution)/shard_map/all_gather | solution.py:37
  110.0 2.3 fusion.9
  112.4 2.2 fusion.5
  114.6 60.3 %all-gather.5.cloned.1.call-done = bf16[160,6144]{1,0:T(8,128)(2,1)} async-done(((bf16[160,384]{1,0:T(8,128)(2,1)}), bf16[160,6144]{1,0:T(8,128)(2,1)}) %all-gather.5.cloned.1.call-update) | async-done | bytes 1966096 | tf_op jit(solution)/shard_map/all_gather | solution.py:38
  174.9 2.2 fusion.1
  178.5 1.6 fusion
  180.1 2.8 copy.40
  182.9 2.2 convolution_convert_fusion
  185.1 2.8 copy.38
  187.9 85.6 %reduce-scatter.9.cloned.1.call-done = bf16[384,160]{1,0:T(8,128)(2,1)} async-done(((bf16[6144,160]{1,0:T(8,128)(2,1)}), bf16[384,160]{1,0:T(8,128)(2,1)}) %reduce-scatter.9.cloned.1.call-update) | async-done | bytes 122896
  273.6 1.1 copy.41
  274.6 93.5 %reduce-scatter.7.cloned.1.call-done = bf16[384,160]{1,0:T(8,128)(2,1)} async-done(((bf16[6144,160]{1,0:T(8,128)(2,1)}), bf16[384,160]{1,0:T(8,128)(2,1)}) %reduce-scatter.7.cloned.1.call-update) | async-done | bytes 122896
  368.1 1.1 copy.39
  369.2 0.8 reshape.67
  370.1 12.8 %all-to-all-start.1 = ((bf16[32,5,768]{2,1,0:T(8,128)(2,1)}), bf16[32,5,768]{2,1,0:T(8,128)(2,1)S(1)}, u32[]{:S(2)}, u32[]{:S(2)}) async-start(bf16[32,5,768]{2,1,0:T(8,128)(2,1)} %reshape.67), calls=%async_computation.1 | async-start | bytes 786432 | tf_op jit(solution)/shard_map/all_to_all | solution.py:68
  383.0 26.5 %all-to-all-done.1 = bf16[32,5,768]{2,1,0:T(8,128)(2,1)S(1)} async-done(((bf16[32,5,768]{2,1,0:T(8,128)(2,1)}), bf16[32,5,768]{2,1,0:T(8,128)(2,1)S(1)}, u32[]{:S(2)}, u32[]{:S(2)}) %all-to-all-start.1) | async-done | bytes 245792 | tf_op jit(solution)/shard_map/all_to_all | solution.py:68
  410.2 38.6 %psum.7 = f32[16,2]{1,0:T(8,128)S(1)} all-reduce(f32[16,2]{1,0:T(8,128)S(1)} %reduce_sum.72), channel_id=1, replica_groups=mesh['pipe'=4,'expert'=32,'tensor'=4] {'pipe','tensor'}, use_global_device_ids=true, to_apply=%region_10.11 | all-reduce | flops 32 | bytes 256 | tf_op jit(solution)/shard_map/psum | solution.py:81
  449.5 0.7 multiply_reduce_fusion.1
  (50 shorter events, 5.8 us)
Async XLA Ops:
  7.2 102.9 %copy-start = (bf16[1,6144,128]{2,1,0:T(8,128)(2,1)S(1)}, bf16[1,6144,128]{2,1,0:T(8,128)(2,1)}, u32[]{:S(2)}) copy-start(bf16[1,6144,128]{2,1,0:T(8,128)(2,1)} %param.10) | copy-start | bytes 4718596
  7.2 102.8 %all-gather.3.cloned.1.call-start = ((), (), s32[]{:S(2)}) async-start(), calls=%async_computation.4 | async-start | bytes 2088960 | tf_op jit(solution)/shard_map/all_gather | solution.py:37
  54.8 120.1 %all-gather.5.cloned.1.call-start = ((), (), s32[]{:S(2)}) async-start(), calls=%async_computation.5 | async-start | bytes 2088960 | tf_op jit(solution)/shard_map/all_gather | solution.py:38
  55.5 218.1 %reduce-scatter.9.cloned.1.call-start = ((), (), s32[]{:S(2)}) async-start(), calls=%async_computation.7 | async-start | bytes 3342336
  110.0 2.4 copy-start.1
  112.4 64.7 %copy-start.4 = (f32[160,128]{1,0:T(8,128)}, f32[160,128]{1,0:T(8,128)S(1)}, u32[]{:S(2)}) copy-start(f32[160,128]{1,0:T(8,128)S(1)} %fusion.9) | copy-start | bytes 245764
  112.4 62.5 %copy-start.2 = (bf16[1,128,6144]{2,1,0:T(8,128)(2,1)S(1)}, bf16[1,128,6144]{2,1,0:T(8,128)(2,1)}, u32[]{:S(2)}) copy-start(bf16[1,128,6144]{2,1,0:T(8,128)(2,1)} %param.12) | copy-start | bytes 4718596
  114.6 62.5 %copy-start.5 = (f32[160,128]{1,0:T(8,128)}, f32[160,128]{1,0:T(8,128)S(1)}, u32[]{:S(2)}) copy-start(f32[160,128]{1,0:T(8,128)S(1)} %fusion.5) | copy-start | bytes 245764
  177.1 1.4 copy-start.3
  182.9 185.2 %reduce-scatter.7.cloned.1.call-start = ((), (), s32[]{:S(2)}) async-start(), calls=%async_computation.6 | async-start | bytes 3342336
  187.9 195.0 %copy-start.7 = (f32[16,2]{0,1:T(2,128)S(1)}, f32[16,2]{0,1:T(2,128)}, u32[]{:S(2)}) copy-start(f32[16,2]{0,1:T(2,128)} %param.9) | copy-start | bytes 388
  187.9 195.1 %copy-start.6 = (bf16[16,384]{1,0:T(8,128)(2,1)S(1)}, bf16[16,384]{1,0:T(8,128)(2,1)}, u32[]{:S(2)}) copy-start(bf16[16,384]{1,0:T(8,128)(2,1)} %param.13) | copy-start | bytes 36868
  370.1 39.5 %all-to-all-start.1 = ((bf16[32,5,768]{2,1,0:T(8,128)(2,1)}), bf16[32,5,768]{2,1,0:T(8,128)(2,1)S(1)}, u32[]{:S(2)}, u32[]{:S(2)}) async-start(bf16[32,5,768]{2,1,0:T(8,128)(2,1)} %reshape.67), calls=%async_computation.1 | async-start | bytes 786432 | tf_op jit(solution)/shard_map/all_to_all | solution.py:68
Sparse Core Ops, SparseCore 0:
  54.9 55.0 all-gather.2
  113.0 61.8 all-gather.4
  183.0 90.5 reduce-scatter.8
  277.6 90.4 reduce-scatter.6
where the time goes:
time: 458 us; the launch traced here: 457 us
  waiting for transfers between devices  321 us (70%)
  blocking collectives  80.5 us (18%)
  between operations  14 us (3%)
  matrix products  13.2 us (3%)
  starting transfers between devices  13 us (3%)
  local copies, waits for them, and re-layouts  12.2 us (3%)
    unnamed x6, waiting for transfers between devices  180 us
    all_gather x1, waiting for transfers between devices, per_device(): rows_dy = lax.all_gather(part_dy, ('pipe', 'tensor'), axis=1, tiled=True)  60.3 us
    all_gather x1, waiting for transfers between devices, per_device(): rows_x = lax.all_gather(part_x, ('pipe', 'tensor'), axis=1, tiled=True)  54.5 us
    all_to_all x1, blocking collectives, per_device(): lax.all_to_all(send, 'expert', split_axis=0, concat_axis=0, tiled=True)  41.8 us
    psum x1, blocking collectives, per_device(): grad_gates = lax.psum(partial_dots, ('pipe', 'tensor'))  38.6 us
    all_to_all x1, waiting for transfers between devices, per_device(): lax.all_to_all(back_send, 'expert', split_axis=0, concat_axis=0, tiled=True)  26.5 us
    all_to_all x1, starting transfers between devices, per_device(): lax.all_to_all(back_send, 'expert', split_axis=0, concat_axis=0, tiled=True)  12.8 us
    unnamed x23, local copies, waits for them, and re-layouts  9.97 us
  transfers between devices with their start and end apart: 5, of which 5 were waited for; matrix products, arithmetic and copies ran while one was open for 2% of the time, Pallas kernels for 0%

commit v1 on v0

--- a/solution.py
+++ b/solution.py
@@ -2,6 +2,14 @@
 import jax.numpy as jnp
 from jax import lax
 from jax.sharding import PartitionSpec as P
+
+draw_frames_on_mesh = lambda frame, mine_x: jnp.split(
+    jax.lax.all_gather(
+        jnp.concatenate([mine_x, frame], axis=0), ("pipe", "tensor"), axis=1, tiled=True
+    ),
+    [mine_x.shape[0]],
+    axis=0,
+)
 
 
 def per_device(tokens, expert_ids, gates, w_gate, w_up, w_down, d_out):
@@ -34,8 +42,7 @@
     recv = recv.reshape(devices_all * capacity, 2 * feat)
     part_x = recv[:, :feat]
     part_dy = recv[:, feat:]
-    rows_x = lax.all_gather(part_x, ("pipe", "tensor"), axis=1, tiled=True)
-    rows_dy = lax.all_gather(part_dy, ("pipe", "tensor"), axis=1, tiled=True)
+    rows_x, rows_dy = draw_frames_on_mesh(part_dy, part_x)
     gate_proj = w_gate[0]
     up_proj = w_up[0]
     down_proj = w_down[0]

time: 458 us -> 405 us (0.88)
  waiting for transfers between devices: 321 us -> 270 us
    all_gather x2 -> x1, waiting for transfers between devices: 115 us -> 64.5 us  [jax.lax.all_gather(jnp.concatenate([mine_x, frame], axis=0), ('pipe', 'te...]
    unnamed x6 -> x5, waiting for transfers between devices: 180 us -> 179 us
  transfers between devices with their start and end apart: 5 -> 4, of which waited for: 5 -> 4; matrix products, arithmetic and copies ran while one was open for 2% -> 2% of each run, Pallas kernels for 0% -> 0%
where the time goes in v1:
time: 405 us; the launch traced here: 404 us
  waiting for transfers between devices  270 us (67%)
  blocking collectives  80.5 us (20%)
  between operations  14 us (3%)
  starting transfers between devices  12.9 us (3%)
  local copies, waits for them, and re-layouts  11.4 us (3%)
  matrix products  11 us (3%)
  other arithmetic  4.13 us (1%)
    unnamed x5, waiting for transfers between devices  179 us
    all_gather x1, waiting for transfers between devices, jax.lax.all_gather(jnp.concatenate([mine_x, frame], axis=0), ('pipe', 'te...  64.5 us
    all_to_all x1, blocking collectives, per_device(): lax.all_to_all(send, 'expert', split_axis=0, concat_axis=0, tiled=True)  41.8 us
    psum x1, blocking collectives, per_device(): grad_gates = lax.psum(partial_dots, ('pipe', 'tensor'))  38.7 us
    all_to_all x1, waiting for transfers between devices, per_device(): lax.all_to_all(back_send, 'expert', split_axis=0, concat_axis=0, tiled=True)  26.5 us
    all_to_all x1, starting transfers between devices, per_device(): lax.all_to_all(back_send, 'expert', split_axis=0, concat_axis=0, tiled=True)  12.8 us
    unnamed x23, local copies, waits for them, and re-layouts  9.88 us
  transfers between devices with their start and end apart: 4, of which 4 were waited for; matrix products, arithmetic and copies ran while one was open for 2% of the time, Pallas kernels for 0%

profile of v1, /device:TPU:32, one launch (start us, length us, event | category | flops | bytes accessed | tf_op | source)
XLA Modules:
  0.0 404.2 jit_solution(18309476877020868811)
XLA Ops:
  7.2 0.9 copy.35
  8.7 0.7 multiply_add_fusion
  9.4 0.8 convert_reduce_fusion
  10.1 0.9 convolution_convert_fusion.1
  11.1 0.9 convolution_convert_fusion.2
  12.1 41.8 %all_to_all.10 = bf16[32,5,768]{2,1,0:T(8,128)(2,1)S(1)} all-to-all(bf16[32,5,768]{2,1,0:T(8,128)(2,1)S(1)} %bitcast.29), channel_id=1, replica_groups=mesh['pipe'=4,'expert'=32,'tensor'=4] {'expert'}, dimensions={0} | all-to-all | bytes 491520 | tf_op jit(solution)/shard_map/all_to_all | solution.py:41
  54.1 0.7 pad_maximum_fusion
  54.9 64.5 %all-gather.2.cloned.1.call-done = bf16[320,6144]{1,0:T(8,128)(2,1)} async-done(((bf16[320,384]{1,0:T(8,128)(2,1)}), bf16[320,6144]{1,0:T(8,128)(2,1)}) %all-gather.2.cloned.1.call-update) | async-done | bytes 3932176 | tf_op jit(solution)/shard_map/all_gather | solution.py:7
  119.3 2.4 fusion.5
  121.7 2.4 fusion.1
  124.1 0.7 fusion.3
  126.1 0.7 fusion
  126.8 2.8 copy.40
  129.7 2.2 convolution_convert_fusion
  131.8 2.8 copy.38
  134.7 85.7 %reduce-scatter.9.cloned.1.call-done = bf16[384,160]{1,0:T(8,128)(2,1)} async-done(((bf16[6144,160]{1,0:T(8,128)(2,1)}), bf16[384,160]{1,0:T(8,128)(2,1)}) %reduce-scatter.9.cloned.1.call-update) | async-done | bytes 122896
  220.3 1.1 copy.41
  221.4 93.6 %reduce-scatter.7.cloned.1.call-done = bf16[384,160]{1,0:T(8,128)(2,1)} async-done(((bf16[6144,160]{1,0:T(8,128)(2,1)}), bf16[384,160]{1,0:T(8,128)(2,1)}) %reduce-scatter.7.cloned.1.call-update) | async-done | bytes 122896
  315.0 1.1 copy.39
  316.1 0.8 reshape.67
  316.9 12.8 %all-to-all-start.1 = ((bf16[32,5,768]{2,1,0:T(8,128)(2,1)}), bf16[32,5,768]{2,1,0:T(8,128)(2,1)S(1)}, u32[]{:S(2)}, u32[]{:S(2)}) async-start(bf16[32,5,768]{2,1,0:T(8,128)(2,1)} %reshape.67), calls=%async_computation.1 | async-start | bytes 786432 | tf_op jit(solution)/shard_map/all_to_all | solution.py:75
  329.9 26.5 %all-to-all-done.1 = bf16[32,5,768]{2,1,0:T(8,128)(2,1)S(1)} async-done(((bf16[32,5,768]{2,1,0:T(8,128)(2,1)}), bf16[32,5,768]{2,1,0:T(8,128)(2,1)S(1)}, u32[]{:S(2)}, u32[]{:S(2)}) %all-to-all-start.1) | async-done | bytes 245792 | tf_op jit(solution)/shard_map/all_to_all | solution.py:75
  357.0 38.7 %psum.7 = f32[16,2]{1,0:T(8,128)S(1)} all-reduce(f32[16,2]{1,0:T(8,128)S(1)} %reduce_sum.72), channel_id=1, replica_groups=mesh['pipe'=4,'expert'=32,'tensor'=4] {'pipe','tensor'}, use_global_device_ids=true, to_apply=%region_10.11 | all-reduce | flops 32 | bytes 256 | tf_op jit(solution)/shard_map/psum | solution.py:88
  396.3 0.7 multiply_reduce_fusion.1
  (48 shorter events, 4.3 us)
Async XLA Ops:
  7.2 112.2 %copy-start = (bf16[1,6144,128]{2,1,0:T(8,128)(2,1)S(1)}, bf16[1,6144,128]{2,1,0:T(8,128)(2,1)}, u32[]{:S(2)}) copy-start(bf16[1,6144,128]{2,1,0:T(8,128)(2,1)} %param.10) | copy-start | bytes 4718596
  7.2 112.1 %all-gather.2.cloned.1.call-start = ((), (), s32[]{:S(2)}) async-start(), calls=%async_computation.4 | async-start | bytes 4177920 | tf_op jit(solution)/shard_map/all_gather | solution.py:7
  54.8 66.9 %copy-start.1 = (bf16[1,128,6144]{2,1,0:T(8,128)(2,1)S(1)}, bf16[1,128,6144]{2,1,0:T(8,128)(2,1)}, u32[]{:S(2)}) copy-start(bf16[1,128,6144]{2,1,0:T(8,128)(2,1)} %param.12) | copy-start | bytes 4718596
  54.8 165.5 %reduce-scatter.9.cloned.1.call-start = ((), (), s32[]{:S(2)}) async-start(), calls=%async_computation.6 | async-start | bytes 3342336
  119.3 4.8 %copy-start.7 = (bf16[320,6144]{1,0:T(8,128)(2,1)S(1)}, bf16[320,6144]{1,0:T(8,128)(2,1)}, u32[]{:S(2)}) copy-start(bf16[320,6144]{1,0:T(8,128)(2,1)} %all-gather.2.cloned.1.call-done) | copy-start | bytes 11796484
  121.7 4.4 %copy-start.3 = (f32[160,128]{1,0:T(8,128)}, f32[160,128]{1,0:T(8,128)S(1)}, u32[]{:S(2)}) copy-start(f32[160,128]{1,0:T(8,128)S(1)} %fusion.5) | copy-start | bytes 245764
  121.7 2.4 copy-start.2
  124.8 0.6 copy-start.4
  129.6 185.4 %reduce-scatter.7.cloned.1.call-start = ((), (), s32[]{:S(2)}) async-start(), calls=%async_computation.5 | async-start | bytes 3342336
  134.6 195.1 %copy-start.6 = (f32[16,2]{0,1:T(2,128)S(1)}, f32[16,2]{0,1:T(2,128)}, u32[]{:S(2)}) copy-start(f32[16,2]{0,1:T(2,128)} %param.9) | copy-start | bytes 388
  134.6 195.2 %copy-start.5 = (bf16[16,384]{1,0:T(8,128)(2,1)S(1)}, bf16[16,384]{1,0:T(8,128)(2,1)}, u32[]{:S(2)}) copy-start(bf16[16,384]{1,0:T(8,128)(2,1)} %param.13) | copy-start | bytes 36868
  316.9 39.5 %all-to-all-start.1 = ((bf16[32,5,768]{2,1,0:T(8,128)(2,1)}), bf16[32,5,768]{2,1,0:T(8,128)(2,1)S(1)}, u32[]{:S(2)}, u32[]{:S(2)}) async-start(bf16[32,5,768]{2,1,0:T(8,128)(2,1)} %reshape.67), calls=%async_computation.1 | async-start | bytes 786432 | tf_op jit(solution)/shard_map/all_to_all | solution.py:75
Sparse Core Ops, SparseCore 0:
  54.9 64.3 all-gather.1
  129.7 90.5 reduce-scatter.8
  224.5 90.4 reduce-scatter.6
